TPU v7x, 256 devices: a whole 4x4x8 slice. The times are simulated.
256 devices in a mesh: cache: 8 (over y, core), dev: 32 (over x, z).
Axes of the slice: x: 4, y: 4, z: 8, core: 2. Of those that a mesh axis runs over, the one named last changes fastest.
Arguments:
- queries: bfloat16 [8, 1024, 8192], P('cache', None, 'dev'), may hold values from -8 to 8
- store_kv: bfloat16 [256, 512, 2048], P('cache', 'dev'), may hold values from -4 to 4
- self_kv: bfloat16 [8, 1024, 2048], P('cache'), may hold values from -5 to 5
- rec_states: bfloat16 [8, 512, 8192], P('cache', None, 'dev'), may hold values from -400 to 400
- norm_gain: bfloat16 [8192], P('dev'), may hold values from 0.099609375 to 1.8984375
- w_kv: bfloat16 [8192, 2048], P('dev'), may hold values from -0.0625 to 0.0625
- retrieval: int32 [8, 16], replicated, may hold values from 0 to 255, as said below
- doc_home: int32 [256], replicated, may hold values from 0 to 255, as said below
- rec_index: int32 [8, 16, 32], P('cache'), may hold values from 0 to 511, as said below
Outputs:
- attended: bfloat16 [8, 1024, 8192], P('cache', None, 'dev')
Inputs may be any that keep to these rules, and one draw needn't show every extreme that they name: `retrieval`: each request names 16 distinct documents; their store rows lie in exactly 4 of the groups of 32 consecutive rows, 4 in each. `doc_home`: every store row holds exactly one document. `rec_index`: the 32 positions of one block are distinct.
All inputs are finite; a program needn't handle non-finite values.
Results may differ from a plain program's by a relative error of at most 0.0045.
Values may be sent and summed in bfloat16 or wider, within the bound.
No kernel may reach another device: no remote copies, remote signals or barrier semaphores. Data moves between devices by JAX's collectives and lax.ppermute only.
A program may use at most 128 MiB of HBM per device.

v0:
```python
import math
import jax
import jax.numpy as jnp
from jax import lax
from jax.sharding import PartitionSpec as P

D = 8192
QH = 64
KVH = 8
HD = 128
RET = 16
CAP = 4
REC = 32
DOC_GRP = 32
eps_norm = 1e-05
tile_rows = 512


def own_head(wide_rows, head_count, head_size, chosen):
    shaped = wide_rows.reshape(wide_rows.shape[:-1] + (2, head_count, head_size))
    taken = lax.dynamic_index_in_dim(shaped, chosen, shaped.ndim - 2, keepdims=False)
    return taken.reshape(wide_rows.shape[:-1] + (2 * head_size,))


def pick_heads(wide_rows, head_count, head_size, chosen):
    shaped = wide_rows.reshape(wide_rows.shape[:-1] + (2, head_count, head_size))
    taken = jnp.take(shaped, chosen, axis=shaped.ndim - 2)
    moved = jnp.moveaxis(taken, shaped.ndim - 2, 0)
    return moved.reshape(moved.shape[:-2] + (2 * head_size,))


def shards(queries, store_kv, self_kv, rec_states, norm_gain, w_kv, retrieval, doc_home, rec_index):
    groups = lax.axis_size("cache")
    members = lax.axis_size("dev")
    my_group = lax.axis_index("cache")
    my_member = lax.axis_index("dev")
    per_device = QH // members
    ratio_heads = QH // KVH
    my_head = my_member * per_device // ratio_heads
    shard_rows = store_kv.shape[1]
    kv_width = store_kv.shape[2]
    inv_root = 1.0 / math.sqrt(HD)
    stored_at = jnp.take(doc_home, retrieval, axis=0)
    source = stored_at // DOC_GRP
    local_row = stored_at % DOC_GRP
    before = jnp.arange(RET)[None, :] < jnp.arange(RET)[:, None]
    same_home = source[:, :, None] == source[:, None, :]
    rank_within = jnp.sum((same_home & before[None, :, :]).astype(jnp.int32), axis=2)
    places = jnp.arange(CAP, dtype=jnp.int32)
    matching = (source[:, None, :] == my_group) & (rank_within[:, None, :] == places[None, :, None])
    pick_row = jnp.sum(jnp.where(matching, local_row[:, None, :], 0), axis=2)
    filled = jnp.any(matching, axis=2)
    outgoing = jnp.take(store_kv, pick_row.reshape(-1), axis=0).reshape(
        groups, CAP, shard_rows, kv_width
    )
    outgoing = jnp.where(filled[:, :, None, None], outgoing, jnp.zeros((), store_kv.dtype))
    my_source = lax.dynamic_index_in_dim(source, my_group, 0, keepdims=False)
    my_rank = lax.dynamic_index_in_dim(rank_within, my_group, 0, keepdims=False)
    slot_place = my_source * CAP + my_rank
    dest_heads = jnp.arange(members, dtype=jnp.int32) * per_device // ratio_heads
    arrived = lax.all_to_all(outgoing, "cache", split_axis=0, concat_axis=0, tiled=True)
    compact = jnp.take(arrived.reshape(groups * CAP, shard_rows, kv_width), slot_place, axis=0)
    spread = pick_heads(compact, KVH, HD, dest_heads)
    fetched = lax.all_to_all(spread, "dev", split_axis=0, concat_axis=2, tiled=True)[0]
    states = rec_states[0].astype(jnp.float32)
    partial_sq = jnp.sum(states * states, axis=1)
    total_sq = lax.psum(partial_sq, "dev")
    inv_rms = lax.rsqrt(total_sq / D + eps_norm)
    normed = (states * norm_gain.astype(jnp.float32)[None, :] * inv_rms[:, None]).astype(
        jnp.bfloat16
    )
    summed = lax.psum(jnp.dot(normed, w_kv, preferred_element_type=jnp.float32), "dev")
    redone = summed.astype(jnp.bfloat16)
    own_rows = own_head(redone.reshape(RET, REC, kv_width), KVH, HD, my_head)
    full_block = fetched.shape[1]
    positions = rec_index[0]
    onehot = positions[:, :, None] == jnp.arange(full_block, dtype=jnp.int32)[None, None, :]
    placed = jnp.einsum(
        "kib,kic->kbc", onehot.astype(jnp.bfloat16), own_rows, preferred_element_type=jnp.float32
    ).astype(jnp.bfloat16)
    replaced_at = jnp.any(onehot, axis=1)
    blocks = jnp.where(replaced_at[:, :, None], placed, fetched)
    doc_keys = blocks[:, :, :HD].reshape(-1, HD)
    doc_values = blocks[:, :, HD:].reshape(-1, HD)
    own_self = own_head(self_kv[0], KVH, HD, my_head)
    self_keys = own_self[:, :HD]
    self_values = own_self[:, HD:]
    prompt = queries.shape[1]
    head_rows = jnp.transpose(queries[0].reshape(prompt, per_device, HD), (1, 0, 2))
    block_len = min(tile_rows, prompt)
    block_count = prompt // block_len
    key_spots = jnp.arange(prompt, dtype=jnp.int32)

    def attend(pair_index):
        head_at = pair_index // block_count
        first_row = pair_index % block_count * block_len
        query_block = lax.dynamic_slice_in_dim(
            lax.dynamic_index_in_dim(head_rows, head_at, 0, keepdims=False), first_row, block_len, 0
        )
        doc_scores = (
            jnp.einsum("qd,kd->qk", query_block, doc_keys, preferred_element_type=jnp.float32)
            * inv_root
        )
        self_scores = (
            jnp.einsum("qd,kd->qk", query_block, self_keys, preferred_element_type=jnp.float32)
            * inv_root
        )
        allowed = (
            key_spots[None, :] <= (first_row + jnp.arange(block_len, dtype=jnp.int32))[:, None]
        )
        self_scores = jnp.where(allowed, self_scores, -jnp.inf)
        top = jnp.maximum(jnp.max(doc_scores, axis=1), jnp.max(self_scores, axis=1))
        doc_expd = jnp.exp(doc_scores - top[:, None])
        self_expd = jnp.exp(self_scores - top[:, None])
        total = jnp.sum(doc_expd, axis=1) + jnp.sum(self_expd, axis=1)
        weighted = jnp.dot(
            doc_expd.astype(jnp.bfloat16), doc_values, preferred_element_type=jnp.float32
        )
        weighted = weighted + jnp.dot(
            self_expd.astype(jnp.bfloat16), self_values, preferred_element_type=jnp.float32
        )
        return (weighted / total[:, None]).astype(jnp.bfloat16)

    gathered_out = lax.map(attend, jnp.arange(per_device * block_count, dtype=jnp.int32))
    result = jnp.transpose(gathered_out.reshape(per_device, prompt, HD), (1, 0, 2))
    return result.reshape(1, prompt, per_device * HD)


def solution(mesh):
    placed = (
        P("cache", None, "dev"),
        P("cache", "dev", None),
        P("cache", None, None),
        P("cache", None, "dev"),
        P("dev"),
        P("dev", None),
        P(),
        P(),
        P("cache", None, None),
    )
    return jax.shard_map(
        shards, mesh=mesh, in_specs=placed, out_specs=P("cache", None, "dev"), check_vma=False
    )
```

profile of v0, /device:TPU:8, one launch (start us, length us, event | category | flops | bytes accessed | tf_op | source)
XLA Modules:
  0.0 544.8 jit_solution(9324490959831772054)
XLA Ops:
  5.4 3.2 select_select_fusion
  8.6 5.7 %all-to-all-start = ((bf16[8,4,16,2048]{3,2,1,0:T(8,128)(2,1)}), bf16[8,4,16,2048]{3,2,1,0:T(8,128)(2,1)S(1)}, u32[]{:S(2)}, u32[]{:S(2)}) async-start(bf16[8,4,16,2048]{3,2,1,0:T(8,128)(2,1)} %select_select_fusion), calls=%async_computation | async-start | bytes 4194304 | tf_op jit(solution)/shard_map/all_to_all | solution.py:61
  14.4 25.7 %all-to-all-done = bf16[8,4,16,2048]{3,2,1,0:T(8,128)(2,1)S(1)} async-done(((bf16[8,4,16,2048]{3,2,1,0:T(8,128)(2,1)}), bf16[8,4,16,2048]{3,2,1,0:T(8,128)(2,1)S(1)}, u32[]{:S(2)}, u32[]{:S(2)}) %all-to-all-start) | async-done | bytes 2097184 | tf_op jit(solution)/shard_map/all_to_all | solution.py:61
  41.2 3.4 gather_fusion.3
  44.6 5.6 %copy_bitcast_fusion = bf16[32,16,16,256]{3,2,1,0:T(8,128)(2,1)} fusion(bf16[32,16,16,2,128]{4,2,3,1,0:T(8,128)(2,1)} %gather_fusion.3, pred[32]{0:T(512)(128)(4,1)S(1)} %compare_and_fusion.2), kind=kLoop, calls=%fused_computation.30 | loop fusion | flops 2097152 | bytes 8388640 | tf_op jit(solution)/shard_map/reshape | solution.py:29
  50.2 10.8 %all-to-all-start.1 = ((bf16[32,16,16,256]{3,2,1,0:T(8,128)(2,1)}), bf16[32,16,16,256]{3,2,1,0:T(8,128)(2,1)}, u32[]{:S(2)}, u32[]{:S(2)}) async-start(bf16[32,16,16,256]{3,2,1,0:T(8,128)(2,1)} %copy_bitcast_fusion), calls=%async_computation.1 | async-start | bytes 8388608 | tf_op jit(solution)/shard_map/all_to_all | solution.py:64
  61.1 155.8 %psum.14 = f32[512]{0:T(512)S(1)} all-reduce(f32[512]{0:T(512)S(1)} %fusion.25), channel_id=1, replica_groups=mesh['cache'=8,'dev'=32] {'dev'}, use_global_device_ids=true, to_apply=%region_2.3 | all-reduce | flops 512 | bytes 4096 | tf_op jit(solution)/shard_map/psum | solution.py:67
  219.7 171.5 %all-reduce.1 = bf16[512,2048]{1,0:T(8,128)(2,1)S(1)} all-reduce(f32[512,2048]{1,0:T(8,128)} %fusion.27), channel_id=1, replica_groups=mesh['cache'=8,'dev'=32] {'dev'}, use_global_device_ids=true, to_apply=%region_3.4 | all-reduce | flops 1048576 | bytes 6291456 | tf_op jit(solution)/shard_map/psum | solution.py:72
  393.2 3.5 dynamic-slice_reduce_fusion.1
  396.8 3.6 copy.42
  400.5 3.7 dynamic-slice_reduce_fusion
  413.7 128.2 %while.14 = (s32[]{:T(128)}, bf16[4,512,128]{2,1,0:T(8,128)(2,1)}, s32[4]{0:T(128)S(1)}, bf16[2,1024,128]{1,2,0:T(8,128)(2,1)S(1)}, bf16[8192,128]{1,0:T(8,128)(...) while((s32[]{:T(128)}, bf16[4,512,128]{2,1,0:T(8,128)(2,1)}, ...), condition=%wide.region_12.13_spmd.clone, body=%wide.region_7.12_spmd.clone.sunk | while | flops 2453863936 | bytes 63343596 | solution.py:124
  417.2 9.9 %multiply_reduce_fusion.2 = (f32[512]{0:T(512)S(1)}, f32[512,8192]{1,0:T(8,128)}) fusion(bf16[8192,128]{1,0:T(8,128)(2,1)} %get-tuple-element.316, bf16[2,1024,128]{1,2,0:T(8,128)(2,1)S(1)} %get-tuple-element.315, s32[]{:T(128)S(6)} %select_n.272, s32[]{:T(128)S(6)} %select_n.275), kind=kOutput, calls=%fused_computation.6.clone.1 | convolution fusion | flops 1082129920 | bytes 19007496 | tf_op jit(solution)/shard_map/while/body/eval_jaxpr/qd,kd->qk/dot_general | solution.py:101
  428.4 8.6 %fusion.70 = f32[512]{0:T(512)S(1)} fusion(f32[512,8192]{1,0:T(8,128)} %get-tuple-element.280, f32[512]{0:T(512)S(1)} %max.13), kind=kLoop, calls=%fused_computation.7.clone.1 | loop fusion | flops 12582400 | bytes 16781312 | tf_op jit(solution)/shard_map/while/body/eval_jaxpr/reduce_sum | solution.py:115
  437.0 7.6 %fusion.69 = f32[512,128]{1,0:T(8,128)S(1)} fusion(bf16[8192,128]{1,0:T(8,128)(2,1)S(1)} %get-tuple-element.318, f32[512,8192]{1,0:T(8,128)} %get-tuple-element.280, f32[512]{0:T(512)S(1)} %max.13), kind=kOutput, calls=%fused_computation.9.clone.1 | convolution fusion | flops 1086324736 | bytes 19138560 | tf_op jit(solution)/shard_map/while/body/eval_jaxpr/dot_general | solution.py:116
  449.2 9.9 %multiply_reduce_fusion.2 = (f32[512]{0:T(512)S(1)}, f32[512,8192]{1,0:T(8,128)}) fusion(bf16[8192,128]{1,0:T(8,128)(2,1)} %get-tuple-element.316, bf16[2,1024,128]{1,2,0:T(8,128)(2,1)S(1)} %get-tuple-element.315, s32[]{:T(128)S(6)} %select_n.272, s32[]{:T(128)S(6)} %select_n.275), kind=kOutput, calls=%fused_computation.6.clone.1 | convolution fusion | flops 1082129920 | bytes 19007496 | tf_op jit(solution)/shard_map/while/body/eval_jaxpr/qd,kd->qk/dot_general | solution.py:101
  460.4 8.6 %fusion.70 = f32[512]{0:T(512)S(1)} fusion(f32[512,8192]{1,0:T(8,128)} %get-tuple-element.280, f32[512]{0:T(512)S(1)} %max.13), kind=kLoop, calls=%fused_computation.7.clone.1 | loop fusion | flops 12582400 | bytes 16781312 | tf_op jit(solution)/shard_map/while/body/eval_jaxpr/reduce_sum | solution.py:115
  469.0 7.6 %fusion.69 = f32[512,128]{1,0:T(8,128)S(1)} fusion(bf16[8192,128]{1,0:T(8,128)(2,1)S(1)} %get-tuple-element.318, f32[512,8192]{1,0:T(8,128)} %get-tuple-element.280, f32[512]{0:T(512)S(1)} %max.13), kind=kOutput, calls=%fused_computation.9.clone.1 | convolution fusion | flops 1086324736 | bytes 19138560 | tf_op jit(solution)/shard_map/while/body/eval_jaxpr/dot_general | solution.py:116
  481.3 9.9 %multiply_reduce_fusion.2 = (f32[512]{0:T(512)S(1)}, f32[512,8192]{1,0:T(8,128)}) fusion(bf16[8192,128]{1,0:T(8,128)(2,1)} %get-tuple-element.316, bf16[2,1024,128]{1,2,0:T(8,128)(2,1)S(1)} %get-tuple-element.315, s32[]{:T(128)S(6)} %select_n.272, s32[]{:T(128)S(6)} %select_n.275), kind=kOutput, calls=%fused_computation.6.clone.1 | convolution fusion | flops 1082129920 | bytes 19007496 | tf_op jit(solution)/shard_map/while/body/eval_jaxpr/qd,kd->qk/dot_general | solution.py:101
  492.5 8.6 %fusion.70 = f32[512]{0:T(512)S(1)} fusion(f32[512,8192]{1,0:T(8,128)} %get-tuple-element.280, f32[512]{0:T(512)S(1)} %max.13), kind=kLoop, calls=%fused_computation.7.clone.1 | loop fusion | flops 12582400 | bytes 16781312 | tf_op jit(solution)/shard_map/while/body/eval_jaxpr/reduce_sum | solution.py:115
  501.1 7.6 %fusion.69 = f32[512,128]{1,0:T(8,128)S(1)} fusion(bf16[8192,128]{1,0:T(8,128)(2,1)S(1)} %get-tuple-element.318, f32[512,8192]{1,0:T(8,128)} %get-tuple-element.280, f32[512]{0:T(512)S(1)} %max.13), kind=kOutput, calls=%fused_computation.9.clone.1 | convolution fusion | flops 1086324736 | bytes 19138560 | tf_op jit(solution)/shard_map/while/body/eval_jaxpr/dot_general | solution.py:116
  513.3 9.9 %multiply_reduce_fusion.2 = (f32[512]{0:T(512)S(1)}, f32[512,8192]{1,0:T(8,128)}) fusion(bf16[8192,128]{1,0:T(8,128)(2,1)} %get-tuple-element.316, bf16[2,1024,128]{1,2,0:T(8,128)(2,1)S(1)} %get-tuple-element.315, s32[]{:T(128)S(6)} %select_n.272, s32[]{:T(128)S(6)} %select_n.275), kind=kOutput, calls=%fused_computation.6.clone.1 | convolution fusion | flops 1082129920 | bytes 19007496 | tf_op jit(solution)/shard_map/while/body/eval_jaxpr/qd,kd->qk/dot_general | solution.py:101
  524.5 8.6 %fusion.70 = f32[512]{0:T(512)S(1)} fusion(f32[512,8192]{1,0:T(8,128)} %get-tuple-element.280, f32[512]{0:T(512)S(1)} %max.13), kind=kLoop, calls=%fused_computation.7.clone.1 | loop fusion | flops 12582400 | bytes 16781312 | tf_op jit(solution)/shard_map/while/body/eval_jaxpr/reduce_sum | solution.py:115
  533.2 7.6 %fusion.69 = f32[512,128]{1,0:T(8,128)S(1)} fusion(bf16[8192,128]{1,0:T(8,128)(2,1)S(1)} %get-tuple-element.318, f32[512,8192]{1,0:T(8,128)} %get-tuple-element.280, f32[512]{0:T(512)S(1)} %max.13), kind=kOutput, calls=%fused_computation.9.clone.1 | convolution fusion | flops 1086324736 | bytes 19138560 | tf_op jit(solution)/shard_map/while/body/eval_jaxpr/dot_general | solution.py:116
  (99 shorter events, 36.6 us)
Async XLA Ops:
  0.0 3.4 copy-start
  0.0 0.9 copy-start.2
  1.0 1.4 copy-start.7
  8.6 31.5 %all-to-all-start = ((bf16[8,4,16,2048]{3,2,1,0:T(8,128)(2,1)}), bf16[8,4,16,2048]{3,2,1,0:T(8,128)(2,1)S(1)}, u32[]{:S(2)}, u32[]{:S(2)}) async-start(bf16[8,4,16,2048]{3,2,1,0:T(8,128)(2,1)} %select_select_fusion), calls=%async_computation | async-start | bytes 4194304 | tf_op jit(solution)/shard_map/all_to_all | solution.py:61
  50.1 10.8 %copy-start.9 = (bf16[256]{0:T(256)(128)(2,1)S(1)}, bf16[256]{0:T(256)(128)(2,1)}, u32[]{:S(2)}) copy-start(bf16[256]{0:T(256)(128)(2,1)} %param.15) | copy-start | bytes 1540
  50.1 10.8 %copy-start.3 = (bf16[1,512,256]{2,1,0:T(8,128)(2,1)S(1)}, bf16[1,512,256]{2,1,0:T(8,128)(2,1)}, u32[]{:S(2)}) copy-start(bf16[1,512,256]{2,1,0:T(8,128)(2,1)} %param.14) | copy-start | bytes 786436
  50.1 166.8 %copy-start.4 = (bf16[256,2048]{1,0:T(8,128)(2,1)S(1)}, bf16[256,2048]{1,0:T(8,128)(2,1)}, u32[]{:S(2)}) copy-start(bf16[256,2048]{1,0:T(8,128)(2,1)} %param.16) | copy-start | bytes 3145732
  50.2 355.5 %all-to-all-start.1 = ((bf16[32,16,16,256]{3,2,1,0:T(8,128)(2,1)}), bf16[32,16,16,256]{3,2,1,0:T(8,128)(2,1)}, u32[]{:S(2)}, u32[]{:S(2)}) async-start(bf16[32,16,16,256]{3,2,1,0:T(8,128)(2,1)} %copy_bitcast_fusion), calls=%async_computation.1 | async-start | bytes 8388608 | tf_op jit(solution)/shard_map/all_to_all | solution.py:64
  400.4 3.8 copy-start.5
  400.5 4.0 copy-start.8
  417.2 9.9 %copy-start.6 = (bf16[1024,128]{1,0:T(8,128)(2,1)S(1)}, bf16[1024,128]{1,0:T(8,128)(2,1)}, u32[]{:S(2)}) copy-start(bf16[1024,128]{1,0:T(8,128)(2,1)} %get-tuple-element.317) | copy-start | bytes 786436 | tf_op jit(solution)/shard_map/while
  449.2 9.9 %copy-start.6 = (bf16[1024,128]{1,0:T(8,128)(2,1)S(1)}, bf16[1024,128]{1,0:T(8,128)(2,1)}, u32[]{:S(2)}) copy-start(bf16[1024,128]{1,0:T(8,128)(2,1)} %get-tuple-element.317) | copy-start | bytes 786436 | tf_op jit(solution)/shard_map/while
  481.3 9.9 %copy-start.6 = (bf16[1024,128]{1,0:T(8,128)(2,1)S(1)}, bf16[1024,128]{1,0:T(8,128)(2,1)}, u32[]{:S(2)}) copy-start(bf16[1024,128]{1,0:T(8,128)(2,1)} %get-tuple-element.317) | copy-start | bytes 786436 | tf_op jit(solution)/shard_map/while
  513.3 9.9 %copy-start.6 = (bf16[1024,128]{1,0:T(8,128)(2,1)S(1)}, bf16[1024,128]{1,0:T(8,128)(2,1)}, u32[]{:S(2)}) copy-start(bf16[1024,128]{1,0:T(8,128)(2,1)} %get-tuple-element.317) | copy-start | bytes 786436 | tf_op jit(solution)/shard_map/while
  541.9 2.9 copy-start.1
where the time goes:
time: 546 us; the launch traced here: 545 us
  blocking collectives  327 us (60%)
  matrix products  83.4 us (15%)
  other arithmetic  47.7 us (9%)
  local copies, waits for them, and re-layouts  32.7 us (6%)
  waiting for transfers between devices  25.7 us (5%)
  starting transfers between devices  16.5 us (3%)
  loops' own time  11.3 us (2%)
    psum x1, blocking collectives, shards(): lax.psum(jnp.dot(normed, w_kv, preferred_element_type=jnp.float32), 'dev')  171 us
    psum x1, blocking collectives, shards(): total_sq = lax.psum(partial_sq, 'dev')  156 us
    dot_general x4, matrix products, attend(): jnp.einsum('qd,kd->qk', query_block, doc_keys, preferred_element_type=jnp...  39.4 us
    reduce_sum x8, other arithmetic, attend(): total = jnp.sum(doc_expd, axis=1) + jnp.sum(self_expd, axis=1)  36.5 us
    dot_general x4, matrix products, attend(): jnp.dot(doc_expd.astype(jnp.bfloat16), doc_values, preferred_element_type...  30.3 us
    all_to_all x1, waiting for transfers between devices, shards(): lax.all_to_all(outgoing, 'cache', split_axis=0, concat_axis=0, tiled=True)  25.7 us
    another operation x1, loops' own time, shards(): lax.map(attend, jnp.arange(per_device * block_count, dtype=jnp.int32))  11.3 us
  transfers between devices with their start and end apart: 2, of which 1 were waited for; matrix products, arithmetic and copies ran while one was open for 3% of the time, Pallas kernels for 0%

commit v1 on v0

--- a/solution.py
+++ b/solution.py
@@ -64,7 +64,7 @@
     fetched = lax.all_to_all(spread, "dev", split_axis=0, concat_axis=2, tiled=True)[0]
     states = rec_states[0].astype(jnp.float32)
     partial_sq = jnp.sum(states * states, axis=1)
-    total_sq = lax.psum(partial_sq, "dev")
+    total_sq = jnp.sum(lax.all_gather(partial_sq, "dev"), axis=0)
     inv_rms = lax.rsqrt(total_sq / D + eps_norm)
     normed = (states * norm_gain.astype(jnp.float32)[None, :] * inv_rms[:, None]).astype(
         jnp.bfloat16

time: 546 us -> 528 us (0.967)
  blocking collectives: 327 us -> 309 us
    psum x1 -> x0, blocking collectives: 156 us -> none  [shards(): total_sq = lax.psum(partial_sq, 'dev')]
    all_gather x0 -> x1, blocking collectives: none -> 135 us  [shards(): total_sq = jnp.sum(lax.all_gather(partial_sq, 'dev'), axis=0)]
where the time goes in v1:
time: 528 us; the launch traced here: 527 us
  blocking collectives  309 us (59%)
  matrix products  83.4 us (16%)
  other arithmetic  47.8 us (9%)
  local copies, waits for them, and re-layouts  32.7 us (6%)
  waiting for transfers between devices  25.7 us (5%)
  starting transfers between devices  16.5 us (3%)
  loops' own time  11.3 us (2%)
    psum x1, blocking collectives, shards(): lax.psum(jnp.dot(normed, w_kv, preferred_element_type=jnp.float32), 'dev')  175 us
    all_gather x1, blocking collectives, shards(): total_sq = jnp.sum(lax.all_gather(partial_sq, 'dev'), axis=0)  135 us
    dot_general x4, matrix products, attend(): jnp.einsum('qd,kd->qk', query_block, doc_keys, preferred_element_type=jnp...  39.4 us
    reduce_sum x8, other arithmetic, attend(): total = jnp.sum(doc_expd, axis=1) + jnp.sum(self_expd, axis=1)  36.5 us
    dot_general x4, matrix products, attend(): jnp.dot(doc_expd.astype(jnp.bfloat16), doc_values, preferred_element_type...  30.3 us
    all_to_all x1, waiting for transfers between devices, shards(): lax.all_to_all(outgoing, 'cache', split_axis=0, concat_axis=0, tiled=True)  25.7 us
    another operation x1, loops' own time, shards(): lax.map(attend, jnp.arange(per_device * block_count, dtype=jnp.int32))  11.3 us
    all_to_all x1, starting transfers between devices, shards(): lax.all_to_all(spread, 'dev', split_axis=0, concat_axis=2, tiled=True)[0]  10.8 us
  transfers between devices with their start and end apart: 2, of which 1 were waited for; matrix products, arithmetic and copies ran while one was open for 3% of the time, Pallas kernels for 0%

profile of v1, /device:TPU:8, one launch (start us, length us, event | category | flops | bytes accessed | tf_op | source)
XLA Modules:
  0.0 526.6 jit_solution(7873913223800622854)
XLA Ops:
  5.4 3.2 select_select_fusion
  8.6 5.7 %all-to-all-start = ((bf16[8,4,16,2048]{3,2,1,0:T(8,128)(2,1)}), bf16[8,4,16,2048]{3,2,1,0:T(8,128)(2,1)S(1)}, u32[]{:S(2)}, u32[]{:S(2)}) async-start(bf16[8,4,16,2048]{3,2,1,0:T(8,128)(2,1)} %select_select_fusion), calls=%async_computation | async-start | bytes 4194304 | tf_op jit(solution)/shard_map/all_to_all | solution.py:61
  14.4 25.7 %all-to-all-done = bf16[8,4,16,2048]{3,2,1,0:T(8,128)(2,1)S(1)} async-done(((bf16[8,4,16,2048]{3,2,1,0:T(8,128)(2,1)}), bf16[8,4,16,2048]{3,2,1,0:T(8,128)(2,1)S(1)}, u32[]{:S(2)}, u32[]{:S(2)}) %all-to-all-start) | async-done | bytes 2097184 | tf_op jit(solution)/shard_map/all_to_all | solution.py:61
  41.2 3.4 gather_fusion.3
  44.6 5.6 %copy_bitcast_fusion = bf16[32,16,16,256]{3,2,1,0:T(8,128)(2,1)} fusion(bf16[32,16,16,2,128]{4,2,3,1,0:T(8,128)(2,1)} %gather_fusion.3, pred[32]{0:T(512)(128)(4,1)S(1)} %compare_and_fusion.2), kind=kLoop, calls=%fused_computation.30 | loop fusion | flops 2097152 | bytes 8388640 | tf_op jit(solution)/shard_map/reshape | solution.py:29
  50.2 10.8 %all-to-all-start.1 = ((bf16[32,16,16,256]{3,2,1,0:T(8,128)(2,1)}), bf16[32,16,16,256]{3,2,1,0:T(8,128)(2,1)}, u32[]{:S(2)}, u32[]{:S(2)}) async-start(bf16[32,16,16,256]{3,2,1,0:T(8,128)(2,1)} %copy_bitcast_fusion), calls=%async_computation.1 | async-start | bytes 8388608 | tf_op jit(solution)/shard_map/all_to_all | solution.py:64
  61.1 134.5 %all-gather.1 = f32[32,1,512]{2,1,0:T(1,128)S(1)} all-gather(f32[1,1,512]{2,1,0:T(1,128)S(1)} %bitcast.111), channel_id=2, replica_groups=mesh['cache'=8,'dev'=32] {'dev'}, dimensions={0}, use_global_device_ids=true | all-gather | bytes 67584 | tf_op jit(solution)/shard_map/all_gather | solution.py:67
  198.5 174.5 %all-reduce.1 = bf16[512,2048]{1,0:T(8,128)(2,1)S(1)} all-reduce(f32[512,2048]{1,0:T(8,128)} %fusion.27), channel_id=1, replica_groups=mesh['cache'=8,'dev'=32] {'dev'}, use_global_device_ids=true, to_apply=%region_3.4 | all-reduce | flops 1048576 | bytes 6291456 | tf_op jit(solution)/shard_map/psum | solution.py:72
  375.1 3.5 dynamic-slice_reduce_fusion.1
  378.7 3.6 copy.50
  382.3 3.7 dynamic-slice_reduce_fusion
  395.5 128.2 %while.14 = (s32[]{:T(128)}, bf16[4,512,128]{2,1,0:T(8,128)(2,1)}, s32[4]{0:T(128)S(1)}, bf16[2,1024,128]{1,2,0:T(8,128)(2,1)S(1)}, bf16[8192,128]{1,0:T(8,128)(...) while((s32[]{:T(128)}, bf16[4,512,128]{2,1,0:T(8,128)(2,1)}, ...), condition=%wide.region_12.13_spmd.clone, body=%wide.region_7.12_spmd.clone.sunk | while | flops 2453863936 | bytes 63343596 | solution.py:124
  399.0 9.9 %multiply_reduce_fusion.2 = (f32[512]{0:T(512)S(1)}, f32[512,8192]{1,0:T(8,128)}) fusion(bf16[8192,128]{1,0:T(8,128)(2,1)} %get-tuple-element.324, bf16[2,1024,128]{1,2,0:T(8,128)(2,1)S(1)} %get-tuple-element.323, s32[]{:T(128)S(6)} %select_n.272, s32[]{:T(128)S(6)} %select_n.275), kind=kOutput, calls=%fused_computation.6.clone.1 | convolution fusion | flops 1082129920 | bytes 19007496 | tf_op jit(solution)/shard_map/while/body/eval_jaxpr/qd,kd->qk/dot_general | solution.py:101
  410.2 8.6 %fusion.70 = f32[512]{0:T(512)S(1)} fusion(f32[512,8192]{1,0:T(8,128)} %get-tuple-element.288, f32[512]{0:T(512)S(1)} %max.13), kind=kLoop, calls=%fused_computation.7.clone.1 | loop fusion | flops 12582400 | bytes 16781312 | tf_op jit(solution)/shard_map/while/body/eval_jaxpr/reduce_sum | solution.py:115
  418.8 7.6 %fusion.69 = f32[512,128]{1,0:T(8,128)S(1)} fusion(bf16[8192,128]{1,0:T(8,128)(2,1)S(1)} %get-tuple-element.326, f32[512,8192]{1,0:T(8,128)} %get-tuple-element.288, f32[512]{0:T(512)S(1)} %max.13), kind=kOutput, calls=%fused_computation.9.clone.1 | convolution fusion | flops 1086324736 | bytes 19138560 | tf_op jit(solution)/shard_map/while/body/eval_jaxpr/dot_general | solution.py:116
  431.1 9.9 %multiply_reduce_fusion.2 = (f32[512]{0:T(512)S(1)}, f32[512,8192]{1,0:T(8,128)}) fusion(bf16[8192,128]{1,0:T(8,128)(2,1)} %get-tuple-element.324, bf16[2,1024,128]{1,2,0:T(8,128)(2,1)S(1)} %get-tuple-element.323, s32[]{:T(128)S(6)} %select_n.272, s32[]{:T(128)S(6)} %select_n.275), kind=kOutput, calls=%fused_computation.6.clone.1 | convolution fusion | flops 1082129920 | bytes 19007496 | tf_op jit(solution)/shard_map/while/body/eval_jaxpr/qd,kd->qk/dot_general | solution.py:101
  442.3 8.6 %fusion.70 = f32[512]{0:T(512)S(1)} fusion(f32[512,8192]{1,0:T(8,128)} %get-tuple-element.288, f32[512]{0:T(512)S(1)} %max.13), kind=kLoop, calls=%fused_computation.7.clone.1 | loop fusion | flops 12582400 | bytes 16781312 | tf_op jit(solution)/shard_map/while/body/eval_jaxpr/reduce_sum | solution.py:115
  450.9 7.6 %fusion.69 = f32[512,128]{1,0:T(8,128)S(1)} fusion(bf16[8192,128]{1,0:T(8,128)(2,1)S(1)} %get-tuple-element.326, f32[512,8192]{1,0:T(8,128)} %get-tuple-element.288, f32[512]{0:T(512)S(1)} %max.13), kind=kOutput, calls=%fused_computation.9.clone.1 | convolution fusion | flops 1086324736 | bytes 19138560 | tf_op jit(solution)/shard_map/while/body/eval_jaxpr/dot_general | solution.py:116
  463.1 9.9 %multiply_reduce_fusion.2 = (f32[512]{0:T(512)S(1)}, f32[512,8192]{1,0:T(8,128)}) fusion(bf16[8192,128]{1,0:T(8,128)(2,1)} %get-tuple-element.324, bf16[2,1024,128]{1,2,0:T(8,128)(2,1)S(1)} %get-tuple-element.323, s32[]{:T(128)S(6)} %select_n.272, s32[]{:T(128)S(6)} %select_n.275), kind=kOutput, calls=%fused_computation.6.clone.1 | convolution fusion | flops 1082129920 | bytes 19007496 | tf_op jit(solution)/shard_map/while/body/eval_jaxpr/qd,kd->qk/dot_general | solution.py:101
  474.3 8.6 %fusion.70 = f32[512]{0:T(512)S(1)} fusion(f32[512,8192]{1,0:T(8,128)} %get-tuple-element.288, f32[512]{0:T(512)S(1)} %max.13), kind=kLoop, calls=%fused_computation.7.clone.1 | loop fusion | flops 12582400 | bytes 16781312 | tf_op jit(solution)/shard_map/while/body/eval_jaxpr/reduce_sum | solution.py:115
  483.0 7.6 %fusion.69 = f32[512,128]{1,0:T(8,128)S(1)} fusion(bf16[8192,128]{1,0:T(8,128)(2,1)S(1)} %get-tuple-element.326, f32[512,8192]{1,0:T(8,128)} %get-tuple-element.288, f32[512]{0:T(512)S(1)} %max.13), kind=kOutput, calls=%fused_computation.9.clone.1 | convolution fusion | flops 1086324736 | bytes 19138560 | tf_op jit(solution)/shard_map/while/body/eval_jaxpr/dot_general | solution.py:116
  495.2 9.9 %multiply_reduce_fusion.2 = (f32[512]{0:T(512)S(1)}, f32[512,8192]{1,0:T(8,128)}) fusion(bf16[8192,128]{1,0:T(8,128)(2,1)} %get-tuple-element.324, bf16[2,1024,128]{1,2,0:T(8,128)(2,1)S(1)} %get-tuple-element.323, s32[]{:T(128)S(6)} %select_n.272, s32[]{:T(128)S(6)} %select_n.275), kind=kOutput, calls=%fused_computation.6.clone.1 | convolution fusion | flops 1082129920 | bytes 19007496 | tf_op jit(solution)/shard_map/while/body/eval_jaxpr/qd,kd->qk/dot_general | solution.py:101
  506.4 8.6 %fusion.70 = f32[512]{0:T(512)S(1)} fusion(f32[512,8192]{1,0:T(8,128)} %get-tuple-element.288, f32[512]{0:T(512)S(1)} %max.13), kind=kLoop, calls=%fused_computation.7.clone.1 | loop fusion | flops 12582400 | bytes 16781312 | tf_op jit(solution)/shard_map/while/body/eval_jaxpr/reduce_sum | solution.py:115
  515.0 7.6 %fusion.69 = f32[512,128]{1,0:T(8,128)S(1)} fusion(bf16[8192,128]{1,0:T(8,128)(2,1)S(1)} %get-tuple-element.326, f32[512,8192]{1,0:T(8,128)} %get-tuple-element.288, f32[512]{0:T(512)S(1)} %max.13), kind=kOutput, calls=%fused_computation.9.clone.1 | convolution fusion | flops 1086324736 | bytes 19138560 | tf_op jit(solution)/shard_map/while/body/eval_jaxpr/dot_general | solution.py:116
  (100 shorter events, 36.7 us)
Async XLA Ops:
  0.0 3.4 copy-start
  0.0 0.9 copy-start.2
  1.0 1.4 copy-start.7
  8.6 31.5 %all-to-all-start = ((bf16[8,4,16,2048]{3,2,1,0:T(8,128)(2,1)}), bf16[8,4,16,2048]{3,2,1,0:T(8,128)(2,1)S(1)}, u32[]{:S(2)}, u32[]{:S(2)}) async-start(bf16[8,4,16,2048]{3,2,1,0:T(8,128)(2,1)} %select_select_fusion), calls=%async_computation | async-start | bytes 4194304 | tf_op jit(solution)/shard_map/all_to_all | solution.py:61
  50.1 10.8 %copy-start.9 = (bf16[256]{0:T(256)(128)(2,1)S(1)}, bf16[256]{0:T(256)(128)(2,1)}, u32[]{:S(2)}) copy-start(bf16[256]{0:T(256)(128)(2,1)} %param.15) | copy-start | bytes 1540
  50.1 10.8 %copy-start.3 = (bf16[1,512,256]{2,1,0:T(8,128)(2,1)S(1)}, bf16[1,512,256]{2,1,0:T(8,128)(2,1)}, u32[]{:S(2)}) copy-start(bf16[1,512,256]{2,1,0:T(8,128)(2,1)} %param.14) | copy-start | bytes 786436
  50.1 145.6 %copy-start.4 = (bf16[256,2048]{1,0:T(8,128)(2,1)S(1)}, bf16[256,2048]{1,0:T(8,128)(2,1)}, u32[]{:S(2)}) copy-start(bf16[256,2048]{1,0:T(8,128)(2,1)} %param.16) | copy-start | bytes 3145732
  50.2 337.3 %all-to-all-start.1 = ((bf16[32,16,16,256]{3,2,1,0:T(8,128)(2,1)}), bf16[32,16,16,256]{3,2,1,0:T(8,128)(2,1)}, u32[]{:S(2)}, u32[]{:S(2)}) async-start(bf16[32,16,16,256]{3,2,1,0:T(8,128)(2,1)} %copy_bitcast_fusion), calls=%async_computation.1 | async-start | bytes 8388608 | tf_op jit(solution)/shard_map/all_to_all | solution.py:64
  382.3 3.8 copy-start.5
  382.3 4.0 copy-start.8
  399.0 9.9 %copy-start.6 = (bf16[1024,128]{1,0:T(8,128)(2,1)S(1)}, bf16[1024,128]{1,0:T(8,128)(2,1)}, u32[]{:S(2)}) copy-start(bf16[1024,128]{1,0:T(8,128)(2,1)} %get-tuple-element.325) | copy-start | bytes 786436 | tf_op jit(solution)/shard_map/while
  431.1 9.9 %copy-start.6 = (bf16[1024,128]{1,0:T(8,128)(2,1)S(1)}, bf16[1024,128]{1,0:T(8,128)(2,1)}, u32[]{:S(2)}) copy-start(bf16[1024,128]{1,0:T(8,128)(2,1)} %get-tuple-element.325) | copy-start | bytes 786436 | tf_op jit(solution)/shard_map/while
  463.1 9.9 %copy-start.6 = (bf16[1024,128]{1,0:T(8,128)(2,1)S(1)}, bf16[1024,128]{1,0:T(8,128)(2,1)}, u32[]{:S(2)}) copy-start(bf16[1024,128]{1,0:T(8,128)(2,1)} %get-tuple-element.325) | copy-start | bytes 786436 | tf_op jit(solution)/shard_map/while
  495.2 9.9 %copy-start.6 = (bf16[1024,128]{1,0:T(8,128)(2,1)S(1)}, bf16[1024,128]{1,0:T(8,128)(2,1)}, u32[]{:S(2)}) copy-start(bf16[1024,128]{1,0:T(8,128)(2,1)} %get-tuple-element.325) | copy-start | bytes 786436 | tf_op jit(solution)/shard_map/while
  523.8 2.9 copy-start.1
